TPU v7x, 256 devices: a whole 4x4x8 slice. The times are simulated.
256 devices in a mesh: group: 4 (over y), shard: 16 (over x_hi, z), tensor: 4 (over x_lo, core).
Axes of the slice: x: 4 (x_hi: 2, x_lo: 2; x = x_hi * 2 + x_lo), y: 4, z: 8, core: 2. Of those that a mesh axis runs over, the one named last changes fastest.
Arguments:
- group_weights: bfloat16 [4, 8, 1024, 8704], P('group', None, None, ('shard', 'tensor')), may hold values from -6 to 6
- anchor: float32 [8, 1024, 16, 4, 136], P(None, ('group', 'shard'), None, 'tensor'), may hold values from -6 to 6
- momentum: float32 [8, 1024, 16, 4, 136], P(None, ('group', 'shard'), None, 'tensor'), may hold values from -6 to 6
- group_embedding: bfloat16 [4, 32000, 1024], P('group', 'shard', 'tensor'), may hold values from -6 to 6
- emb_anchor: float32 [32000, 1024], P('shard', 'tensor'), may hold values from -6 to 6
- emb_momentum: float32 [32000, 1024], P('shard', 'tensor'), may hold values from -6 to 6
- basis: float32 [1024, 64], P('tensor'), may hold values from -0.1875 to 0.1875
Outputs:
- new_weights: bfloat16 [8, 1024, 8704], P(None, None, ('shard', 'tensor'))
- new_anchor: float32 [8, 1024, 16, 4, 136], P(None, ('group', 'shard'), None, 'tensor')
- new_momentum: float32 [8, 1024, 16, 4, 136], P(None, ('group', 'shard'), None, 'tensor')
- new_embedding: bfloat16 [32000, 1024], P('shard', 'tensor')
- new_emb_anchor: float32 [32000, 1024], P('shard', 'tensor')
- new_emb_momentum: float32 [32000, 1024], P('shard', 'tensor')
All inputs are finite; a program needn't handle non-finite values.
Results may differ from a plain program's by a relative error of at most 0.012.
Values may be sent and summed in bfloat16 or wider, within the bound.
No kernel may reach another device: no remote copies, remote signals or barrier semaphores. Data moves between devices by JAX's collectives and lax.ppermute only.
A program may use at most 128 MiB of HBM per device.

v0:
```python
import jax
import jax.numpy as jnp
from jax import lax
from jax.sharding import PartitionSpec as P

outer_rate = 0.7
momentum_decay = 0.9


def per_device(group_weights, anchor, momentum, group_embedding, emb_anchor, emb_momentum, basis):
    groups = lax.axis_size("group")
    layers = group_weights.shape[1]
    width = group_weights.shape[2]
    block = group_weights.shape[3]
    local_weights = group_weights[0]
    part = lax.psum_scatter(
        local_weights.astype(jnp.float32).astype(jnp.bfloat16),
        "group",
        scatter_dimension=1,
        tiled=True,
    ).astype(jnp.float32)
    part = part.reshape(layers, part.shape[1], 1, 1, block)
    summed = lax.all_to_all(part, "shard", split_axis=1, concat_axis=2, tiled=True)
    delta = anchor - summed / groups
    moved = momentum_decay * momentum + delta
    stepped = anchor - outer_rate * (delta + momentum_decay * moved)
    stepped_half = stepped.astype(jnp.bfloat16)
    columns = lax.all_to_all(stepped_half, "shard", split_axis=2, concat_axis=1, tiled=True)
    whole = lax.all_gather(columns, "group", axis=1, tiled=True)
    new_weights = whole.reshape(layers, width, block)
    local_embedding = group_embedding[0].astype(jnp.float32)
    emb_sum = lax.psum(local_embedding.astype(jnp.bfloat16), "group").astype(jnp.float32)
    difference = emb_anchor - emb_sum / groups
    coef = lax.psum(jnp.dot(difference, basis, precision=lax.Precision.HIGHEST), "tensor")
    emb_delta = jnp.dot(coef, basis.T, precision=lax.Precision.HIGHEST)
    emb_moved = momentum_decay * emb_momentum + emb_delta
    emb_stepped = emb_anchor - outer_rate * (emb_delta + momentum_decay * emb_moved)
    return (new_weights, stepped, moved, emb_stepped.astype(jnp.bfloat16), emb_stepped, emb_moved)


def solution(mesh):
    return jax.shard_map(
        per_device,
        mesh=mesh,
        in_specs=(
            P("group", None, None, ("shard", "tensor")),
            P(None, ("group", "shard"), None, "tensor", None),
            P(None, ("group", "shard"), None, "tensor", None),
            P("group", "shard", "tensor"),
            P("shard", "tensor"),
            P("shard", "tensor"),
            P("tensor", None),
        ),
        out_specs=(
            P(None, None, ("shard", "tensor")),
            P(None, ("group", "shard"), None, "tensor", None),
            P(None, ("group", "shard"), None, "tensor", None),
            P("shard", "tensor"),
            P("shard", "tensor"),
            P("shard", "tensor"),
        ),
        check_vma=False,
    )
```

profile of v0, /device:TPU:1, one launch (start us, length us, event | category | flops | bytes accessed | tf_op | source)
XLA Modules:
  0.0 260.1 jit_solution(16609563485341192564)
XLA Ops:
  7.2 0.0 copy-start
  7.2 0.0 reduce-scatter.2.cloned.1.call-start
  7.2 6.8 %copy.20 = bf16[1,8,1024,136]{3,1,2,0:T(8,128)(2,1)} copy(bf16[1,8,1024,136]{2,3,1,0:T(8,128)(2,1)} %param.7) | data formatting | bytes 4456448 | tf_op args[0]
  14.0 0.0 reduce-scatter.2.cloned.1.call-update
  14.0 53.3 %reduce-scatter.2.cloned.1.call-done = bf16[8,256,136]{2,0,1:T(8,128)(2,1)} async-done(((bf16[8,1024,136]{2,0,1:T(8,128)(2,1)}), bf16[8,256,136]{2,0,1:T(8,128)(2,1)}) %reduce-scatter.2.cloned.1.call-update) | async-done | bytes 557072 | tf_op jit(solution)/shard_map/reduce_scatter | solution.py:16
  67.3 2.7 %bitcast_convert_fusion = f32[8,256,1,1,136]{4,0,3,2,1:T(8,128)} fusion(bf16[8,256,136]{2,0,1:T(8,128)(2,1)} %reduce-scatter.2.cloned.1.call-done), kind=kLoop, calls=%fused_computation.11 | loop fusion | flops 278528 | bytes 1671168 | tf_op jit(solution)/shard_map/reshape | solution.py:22
  70.0 9.2 %all-to-all-start = ((f32[8,256,1,1,136]{4,0,3,2,1:T(8,128)}), f32[8,256,1,1,136]{4,0,3,2,1:T(8,128)S(1)}, u32[]{:S(2)}, u32[]{:S(2)}) async-start(f32[8,256,1,1,136]{4,0,3,2,1:T(8,128)} %bitcast_convert_fusion), calls=%async_computation.1 | async-start | bytes 4194304 | tf_op jit(solution)/shard_map/all_to_all | solution.py:23
  79.3 0.0 all-reduce.3.cloned.1.call-start
  79.3 0.7 all-reduce.3.cloned.1.call-update
  80.0 48.4 %all-to-all-done = f32[8,256,1,1,136]{4,0,3,2,1:T(8,128)S(1)} async-done(((f32[8,256,1,1,136]{4,0,3,2,1:T(8,128)}), f32[8,256,1,1,136]{4,0,3,2,1:T(8,128)S(1)}, u32[]{:S(2)}, u32[]{:S(2)}) %all-to-all-start) | async-done | bytes 1114144 | tf_op jit(solution)/shard_map/all_to_all | solution.py:23
  128.5 0.7 copy_multiply_fusion.1
  129.2 0.9 copy-done.2
  130.1 0.6 copy-done.3
  130.7 5.1 %fusion.8 = (bf16[8,16,16,1,136]{4,1,2,0,3:T(8,128)(2,1)S(1)}, f32[8,16,16,1,136]{4,1,2,0,3:T(8,128)}, f32[8,16,16,1,136]{4,1,2,0,3:T(8,128)S(1)}) fusion(f32[8,16,16,1,136]{4,3,2,1,0:T(1,128)S(1)} %copy-done.2, f32[8,16,16,1,136]{4,1,2,0,3:T(8,128)S(1)} %bitcast.19, f32[8,16,16,1,136]{4,3,2,1,0:T(1,128)S(1)} %copy-done.3), kind=kLoop, calls=%fused_computation.15 | loop fusion | flops 2228224 | bytes 6127616 | tf_op jit(solution)/shard_map/convert_element_type | solution.py:27
  135.8 1.1 copy.25
  136.9 7.1 %all-to-all-start.1 = ((bf16[8,16,16,1,136]{4,1,0,3,2:T(8,128)(2,1)}), bf16[8,16,16,1,136]{4,1,0,3,2:T(8,128)(2,1)S(1)}, u32[]{:S(2)}, u32[]{:S(2)}) async-start(bf16[8,16,16,1,136]{4,1,0,3,2:T(8,128)(2,1)} %copy.25), calls=%async_computation.2 | async-start | bytes 2097152 | tf_op jit(solution)/shard_map/all_to_all | solution.py:28
  144.0 0.0 all-reduce.5.cloned.1.call-start
  144.1 0.0 all-reduce.3.cloned.1.call-done
  144.1 0.0 copy-done
  144.1 4.8 %fusion.1 = f32[2000,64]{0,1:T(8,128)} fusion(f32[256,64]{0,1:T(8,128)S(1)} %copy-done, f32[2000,256]{1,0:T(8,128)} %param.11, bf16[2000,256]{1,0:T(8,128)(2,1)} %all-reduce.3.cloned.1.call-done), kind=kOutput, calls=%fused_computation.6 | convolution fusion | flops 394752000 | bytes 3649536 | tf_op jit(solution)/shard_map/dot_general | solution.py:34
  148.9 0.0 all-reduce.5.cloned.1.call-update
  148.9 0.2 all-gather.2.cloned.1.call-start
  149.1 21.9 %all-to-all-done.1 = bf16[8,16,16,1,136]{4,1,0,3,2:T(8,128)(2,1)S(1)} async-done(((bf16[8,16,16,1,136]{4,1,0,3,2:T(8,128)(2,1)}), bf16[8,16,16,1,136]{4,1,0,3,2:T(8,128)(2,1)S(1)}, u32[]{:S(2)}, u32[]{:S(2)}) %all-to-all-start.1) | async-done | bytes 557088 | tf_op jit(solution)/shard_map/all_to_all | solution.py:28
  171.1 1.1 copy.26
  172.2 0.0 all-gather.2.cloned.1.call-update
  172.2 22.1 %all-reduce.5.cloned.1.call-done = f32[2000,64]{0,1:T(8,128)} async-done(((f32[2000,64]{0,1:T(8,128)}), f32[2000,64]{0,1:T(8,128)}) %all-reduce.5.cloned.1.call-update) | async-done | bytes 512016 | tf_op jit(solution)/shard_map/psum | solution.py:34
  194.3 6.9 %fusion.7 = (bf16[2000,256]{1,0:T(8,128)(2,1)}, f32[2000,256]{1,0:T(8,128)}, f32[2000,256]{1,0:T(8,128)}) fusion(f32[2000,256]{1,0:T(8,128)} %param.11, f32[2000,256]{1,0:T(8,128)} %param.12, f32[2000,64]{0,1:T(8,128)} %all-reduce.5.cloned.1.call-done, f32[256,64]{0,1:T(8,128)S(1)} %copy-done), kind=kOutput, calls=%fused_computation.14 | convolution fusion | flops 396800000 | bytes 9793536 | tf_op jit(solution)/shard_map/dot_general | solution.py:35
  201.3 0.0 copy-done.1
  201.3 3.7 %copy.28 = f32[8,16,16,1,136]{4,3,2,1,0:T(1,128)} copy(f32[8,16,16,1,136]{4,1,2,0,3:T(8,128)S(1)} %copy-done.1) | data formatting | bytes 2228224
  205.0 3.7 %copy.29 = f32[8,16,16,1,136]{4,3,2,1,0:T(1,128)} copy(f32[8,16,16,1,136]{4,1,2,0,3:T(8,128)S(1)} %get-tuple-element.23) | data formatting | bytes 2228224
  208.7 39.0 %all-gather.2.cloned.1.call-done = bf16[8,1024,1,1,136]{4,1,0,3,2:T(8,128)(2,1)} async-done(((bf16[8,256,1,1,136]{4,1,0,3,2:T(8,128)(2,1)}), bf16[8,1024,1,1,136]{4,1,0,3,2:T(8,128)(2,1)}) %all-gather.2.cloned.1.call-update) | async-done | bytes 2228240 | tf_op jit(solution)/shard_map/all_gather | solution.py:29
  247.7 5.9 %copy.27 = bf16[8,1024,136]{1,2,0:T(8,128)(2,1)} copy(bf16[8,1024,136]{2,1,0:T(8,128)(2,1)} %bitcast.20) | data formatting | bytes 4456448
  (3 shorter events, 0.0 us)
Async XLA Ops:
  7.2 136.9 %copy-start = (f32[256,64]{0,1:T(8,128)S(1)}, f32[256,64]{0,1:T(8,128)}, u32[]{:S(2)}) copy-start(f32[256,64]{0,1:T(8,128)} %param.13) | copy-start | bytes 196612
  7.2 60.1 %reduce-scatter.2.cloned.1.call-start = ((), (), s32[]{:S(2)}) async-start(), calls=%async_computation.3 | async-start | bytes 5242880 | tf_op jit(solution)/shard_map/reduce_scatter | solution.py:16
  70.0 58.4 %all-to-all-start = ((f32[8,256,1,1,136]{4,0,3,2,1:T(8,128)}), f32[8,256,1,1,136]{4,0,3,2,1:T(8,128)S(1)}, u32[]{:S(2)}, u32[]{:S(2)}) async-start(f32[8,256,1,1,136]{4,0,3,2,1:T(8,128)} %bitcast_convert_fusion), calls=%async_computation.1 | async-start | bytes 4194304 | tf_op jit(solution)/shard_map/all_to_all | solution.py:23
  79.3 64.8 %all-reduce.3.cloned.1.call-start = ((), (), s32[]{:S(2)}) async-start(), calls=%async_computation.5 | async-start | bytes 2048000 | tf_op jit(solution)/shard_map/psum | solution.py:32
  128.5 1.6 copy-start.2
  128.5 2.3 copy-start.3
  136.9 34.2 %all-to-all-start.1 = ((bf16[8,16,16,1,136]{4,1,0,3,2:T(8,128)(2,1)}), bf16[8,16,16,1,136]{4,1,0,3,2:T(8,128)(2,1)S(1)}, u32[]{:S(2)}, u32[]{:S(2)}) async-start(bf16[8,16,16,1,136]{4,1,0,3,2:T(8,128)(2,1)} %copy.25), calls=%async_computation.2 | async-start | bytes 2097152 | tf_op jit(solution)/shard_map/all_to_all | solution.py:28
  144.0 50.3 %all-reduce.5.cloned.1.call-start = ((), (), s32[]{:S(2)}) async-start(), calls=%async_computation.6 | async-start | bytes 1048576 | tf_op jit(solution)/shard_map/psum | solution.py:34
  148.9 98.8 %all-gather.2.cloned.1.call-start = ((), (), s32[]{:S(2)}) async-start(), calls=%async_computation.4 | async-start | bytes 5242880 | tf_op jit(solution)/shard_map/all_gather | solution.py:29
  194.3 6.9 %copy-start.1 = (f32[8,16,16,1,136]{4,1,2,0,3:T(8,128)S(1)}, f32[8,16,16,1,136]{4,1,2,0,3:T(8,128)}, u32[]{:S(2)}) copy-start(f32[8,16,16,1,136]{4,1,2,0,3:T(8,128)} %get-tuple-element.22) | copy-start | bytes 3342340
Sparse Core Ops, SparseCore 0:
  14.1 53.1 reduce-scatter.1
  82.4 50.1 all-reduce.2
  149.0 45.2 all-reduce.4
  196.6 51.0 all-gather.1
where the time goes:
time: 261 us; the launch traced here: 260 us
  waiting for transfers between devices  186 us (71%)
  local copies, waits for them, and re-layouts  23.8 us (9%)
  starting transfers between devices  16.7 us (6%)
  between operations  13.8 us (5%)
  matrix products  11.7 us (4%)
  other arithmetic  8.55 us (3%)
    reduce_scatter x1, waiting for transfers between devices, per_device(): lax.psum_scatter(local_weights.astype(jnp.float32).astype(jnp.bfloat16),...  53.3 us
    all_to_all x1, waiting for transfers between devices, per_device(): lax.all_to_all(part, 'shard', split_axis=1, concat_axis=2, tiled=True)  48.4 us
    all_gather x1, waiting for transfers between devices, per_device(): whole = lax.all_gather(columns, 'group', axis=1, tiled=True)  39 us
    psum x1, waiting for transfers between devices, per_device(): lax.psum(jnp.dot(difference, basis, precision=lax.Precision.HIGHEST), 'te...  22.1 us
    all_to_all x1, waiting for transfers between devices, per_device(): lax.all_to_all(stepped_half, 'shard', split_axis=2, concat_axis=1, tiled=...  21.9 us
    unnamed x12, local copies, waits for them, and re-layouts  21.6 us
    all_to_all x1, starting transfers between devices, per_device(): lax.all_to_all(part, 'shard', split_axis=1, concat_axis=2, tiled=True)  9.24 us
    all_to_all x1, starting transfers between devices, per_device(): lax.all_to_all(stepped_half, 'shard', split_axis=2, concat_axis=1, tiled=...  7.1 us
  transfers between devices with their start and end apart: 6, of which 5 were waited for; matrix products, arithmetic and copies ran while one was open for 10% of the time, Pallas kernels for 0%

commit v1 on v0

--- a/solution.py
+++ b/solution.py
@@ -25,7 +25,12 @@
     moved = momentum_decay * momentum + delta
     stepped = anchor - outer_rate * (delta + momentum_decay * moved)
     stepped_half = stepped.astype(jnp.bfloat16)
-    columns = lax.all_to_all(stepped_half, "shard", split_axis=2, concat_axis=1, tiled=True)
+    columns = jnp.concatenate(
+        lax.all_to_all(
+            jnp.stack(jnp.split(stepped_half, lax.axis_size("shard"), axis=2)), "shard", 0, 0
+        ),
+        axis=1,
+    )
     whole = lax.all_gather(columns, "group", axis=1, tiled=True)
     new_weights = whole.reshape(layers, width, block)
     local_embedding = group_embedding[0].astype(jnp.float32)

time: 261 us -> 270 us (1.034)
  local copies, waits for them, and re-layouts: 23.8 us -> 32.8 us
    unnamed x12 -> x27, local copies, waits for them, and re-layouts: 21.6 us -> 31.1 us
  transfers between devices with their start and end apart: 6 -> 6, of which waited for: 5 -> 5; matrix products, arithmetic and copies ran while one was open for 10% -> 13% of each run, Pallas kernels for 0% -> 0%
where the time goes in v1:
time: 270 us; the launch traced here: 269 us
  waiting for transfers between devices  186 us (69%)
  local copies, waits for them, and re-layouts  32.8 us (12%)
  starting transfers between devices  16.7 us (6%)
  between operations  13.8 us (5%)
  matrix products  11.7 us (4%)
  other arithmetic  8.55 us (3%)
    reduce_scatter x1, waiting for transfers between devices, per_device(): lax.psum_scatter(local_weights.astype(jnp.float32).astype(jnp.bfloat16),...  53.3 us
    all_to_all x1, waiting for transfers between devices, per_device(): lax.all_to_all(part, 'shard', split_axis=1, concat_axis=2, tiled=True)  48.4 us
    all_gather x1, waiting for transfers between devices, per_device(): whole = lax.all_gather(columns, 'group', axis=1, tiled=True)  39 us
    unnamed x27, local copies, waits for them, and re-layouts  31.1 us
    psum x1, waiting for transfers between devices, per_device(): lax.psum(jnp.dot(difference, basis, precision=lax.Precision.HIGHEST), 'te...  22.1 us
    all_to_all x1, waiting for transfers between devices, per_device(): lax.all_to_all(jnp.stack(jnp.split(stepped_half, lax.axis_size('shard'),...  21.9 us
    all_to_all x1, starting transfers between devices, per_device(): lax.all_to_all(part, 'shard', split_axis=1, concat_axis=2, tiled=True)  9.24 us
    all_to_all x1, starting transfers between devices, per_device(): lax.all_to_all(jnp.stack(jnp.split(stepped_half, lax.axis_size('shard'),...  7.1 us
  transfers between devices with their start and end apart: 6, of which 5 were waited for; matrix products, arithmetic and copies ran while one was open for 13% of the time, Pallas kernels for 0%

profile of v1, /device:TPU:1, one launch (start us, length us, event | category | flops | bytes accessed | tf_op | source)
XLA Modules:
  0.0 269.2 jit_solution(12529051423488278)
XLA Ops:
  7.2 6.8 %copy.51 = bf16[1,8,1024,136]{3,1,2,0:T(8,128)(2,1)} copy(bf16[1,8,1024,136]{2,3,1,0:T(8,128)(2,1)} %param.7) | data formatting | bytes 4456448 | tf_op args[0]
  14.0 53.3 %reduce-scatter.2.cloned.1.call-done = bf16[8,256,136]{2,0,1:T(8,128)(2,1)} async-done(((bf16[8,1024,136]{2,0,1:T(8,128)(2,1)}), bf16[8,256,136]{2,0,1:T(8,128)(2,1)}) %reduce-scatter.2.cloned.1.call-update) | async-done | bytes 557072 | tf_op jit(solution)/shard_map/reduce_scatter | solution.py:16
  67.3 2.7 %bitcast_convert_fusion = f32[8,256,1,1,136]{4,0,3,2,1:T(8,128)} fusion(bf16[8,256,136]{2,0,1:T(8,128)(2,1)} %reduce-scatter.2.cloned.1.call-done), kind=kLoop, calls=%fused_computation.11 | loop fusion | flops 278528 | bytes 1671168 | tf_op jit(solution)/shard_map/reshape | solution.py:22
  70.0 9.2 %all-to-all-start = ((f32[8,256,1,1,136]{4,0,3,2,1:T(8,128)}), f32[8,256,1,1,136]{4,0,3,2,1:T(8,128)S(1)}, u32[]{:S(2)}, u32[]{:S(2)}) async-start(f32[8,256,1,1,136]{4,0,3,2,1:T(8,128)} %bitcast_convert_fusion), calls=%async_computation.1 | async-start | bytes 4194304 | tf_op jit(solution)/shard_map/all_to_all | solution.py:23
  79.3 0.7 all-reduce.3.cloned.1.call-update
  80.0 48.4 %all-to-all-done = f32[8,256,1,1,136]{4,0,3,2,1:T(8,128)S(1)} async-done(((f32[8,256,1,1,136]{4,0,3,2,1:T(8,128)}), f32[8,256,1,1,136]{4,0,3,2,1:T(8,128)S(1)}, u32[]{:S(2)}, u32[]{:S(2)}) %all-to-all-start) | async-done | bytes 1114144 | tf_op jit(solution)/shard_map/all_to_all | solution.py:23
  128.5 0.7 copy_multiply_fusion.1
  129.2 0.9 copy-done.2
  130.1 0.6 copy-done.3
  130.7 5.1 %fusion.24 = (bf16[8,16,16,1,136]{4,1,2,0,3:T(8,128)(2,1)S(1)}, f32[8,16,16,1,136]{4,1,2,0,3:T(8,128)}, f32[8,16,16,1,136]{4,1,2,0,3:T(8,128)S(1)}) fusion(f32[8,16,16,1,136]{4,3,2,1,0:T(1,128)S(1)} %copy-done.2, f32[8,16,16,1,136]{4,1,2,0,3:T(8,128)S(1)} %bitcast.111, f32[8,16,16,1,136]{4,3,2,1,0:T(1,128)S(1)} %copy-done.3), kind=kLoop, calls=%fused_computation.47 | loop fusion | flops 2228224 | bytes 6127616 | tf_op jit(solution)/shard_map/convert_element_type | solution.py:27
  135.8 0.6 fusion.21
  136.5 0.6 fusion.20
  137.1 0.6 fusion.19
  137.7 0.6 fusion.18
  138.4 0.6 fusion.17
  139.0 0.6 fusion.16
  139.6 0.6 fusion.15
  140.3 0.6 fusion.14
  140.9 0.6 fusion.13
  141.5 0.6 fusion.12
  142.2 0.6 fusion.11
  142.8 0.6 fusion.10
  146.0 7.1 %all-to-all-start.1 = ((bf16[16,8,16,1,1,136]{5,2,1,4,3,0:T(8,128)(2,1)}), bf16[16,8,16,1,1,136]{5,2,1,4,3,0:T(8,128)(2,1)S(1)}, u32[]{:S(2)}, u32[]{:S(2)}) async-start(bf16[16,8,16,1,1,136]{5,2,1,4,3,0:T(8,128)(2,1)} %fusion.6), calls=%async_computation.2 | async-start | bytes 2097152 | tf_op jit(solution)/shard_map/all_to_all | solution.py:29
  153.2 4.8 %fusion.1 = f32[2000,64]{0,1:T(8,128)} fusion(f32[256,64]{0,1:T(8,128)S(1)} %copy-done, f32[2000,256]{1,0:T(8,128)} %param.11, bf16[2000,256]{1,0:T(8,128)(2,1)} %all-reduce.3.cloned.1.call-done), kind=kOutput, calls=%fused_computation.6 | convolution fusion | flops 394752000 | bytes 3649536 | tf_op jit(solution)/shard_map/dot_general | solution.py:39
  158.2 21.9 %all-to-all-done.1 = bf16[16,8,16,1,1,136]{5,2,1,4,3,0:T(8,128)(2,1)S(1)} async-done(((bf16[16,8,16,1,1,136]{5,2,1,4,3,0:T(8,128)(2,1)}), bf16[16,8,16,1,1,136]{5,2,1,4,3,0:T(8,128)(2,1)S(1)}, u32[]{:S(2)}, u32[]{:S(2)}) %all-to-all-start.1) | async-done | bytes 557088 | tf_op jit(solution)/shard_map/all_to_all | solution.py:29
  180.1 1.1 copy.71
  181.2 22.1 %all-reduce.5.cloned.1.call-done = f32[2000,64]{0,1:T(8,128)} async-done(((f32[2000,64]{0,1:T(8,128)}), f32[2000,64]{0,1:T(8,128)}) %all-reduce.5.cloned.1.call-update) | async-done | bytes 512016 | tf_op jit(solution)/shard_map/psum | solution.py:39
  203.4 6.9 %fusion.23 = (bf16[2000,256]{1,0:T(8,128)(2,1)}, f32[2000,256]{1,0:T(8,128)}, f32[2000,256]{1,0:T(8,128)}) fusion(f32[2000,256]{1,0:T(8,128)} %param.11, f32[2000,256]{1,0:T(8,128)} %param.12, f32[2000,64]{0,1:T(8,128)} %all-reduce.5.cloned.1.call-done, f32[256,64]{0,1:T(8,128)S(1)} %copy-done), kind=kOutput, calls=%fused_computation.46 | convolution fusion | flops 396800000 | bytes 9793536 | tf_op jit(solution)/shard_map/dot_general | solution.py:40
  210.3 3.7 %copy.73 = f32[8,16,16,1,136]{4,3,2,1,0:T(1,128)} copy(f32[8,16,16,1,136]{4,1,2,0,3:T(8,128)S(1)} %copy-done.1) | data formatting | bytes 2228224
  214.0 3.7 %copy.74 = f32[8,16,16,1,136]{4,3,2,1,0:T(1,128)} copy(f32[8,16,16,1,136]{4,1,2,0,3:T(8,128)S(1)} %get-tuple-element.23) | data formatting | bytes 2228224
  217.8 39.0 %all-gather.2.cloned.1.call-done = bf16[8,1024,1,1,136]{4,1,0,3,2:T(8,128)(2,1)} async-done(((bf16[8,256,1,1,136]{4,1,0,3,2:T(8,128)(2,1)}), bf16[8,1024,1,1,136]{4,1,0,3,2:T(8,128)(2,1)}) %all-gather.2.cloned.1.call-update) | async-done | bytes 2228240 | tf_op jit(solution)/shard_map/all_gather | solution.py:34
  256.7 5.9 %copy.72 = bf16[8,1024,136]{1,2,0:T(8,128)(2,1)} copy(bf16[8,1024,136]{2,1,0:T(8,128)(2,1)} %bitcast.112) | data formatting | bytes 4456448
  (18 shorter events, 3.0 us)
Async XLA Ops:
  7.2 146.0 %copy-start = (f32[256,64]{0,1:T(8,128)S(1)}, f32[256,64]{0,1:T(8,128)}, u32[]{:S(2)}) copy-start(f32[256,64]{0,1:T(8,128)} %param.13) | copy-start | bytes 196612
  7.2 60.1 %reduce-scatter.2.cloned.1.call-start = ((), (), s32[]{:S(2)}) async-start(), calls=%async_computation.3 | async-start | bytes 5242880 | tf_op jit(solution)/shard_map/reduce_scatter | solution.py:16
  70.0 58.4 %all-to-all-start = ((f32[8,256,1,1,136]{4,0,3,2,1:T(8,128)}), f32[8,256,1,1,136]{4,0,3,2,1:T(8,128)S(1)}, u32[]{:S(2)}, u32[]{:S(2)}) async-start(f32[8,256,1,1,136]{4,0,3,2,1:T(8,128)} %bitcast_convert_fusion), calls=%async_computation.1 | async-start | bytes 4194304 | tf_op jit(solution)/shard_map/all_to_all | solution.py:23
  79.3 73.9 %all-reduce.3.cloned.1.call-start = ((), (), s32[]{:S(2)}) async-start(), calls=%async_computation.5 | async-start | bytes 2048000 | tf_op jit(solution)/shard_map/psum | solution.py:37
  128.5 1.6 copy-start.2
  128.5 2.3 copy-start.3
  146.0 34.2 %all-to-all-start.1 = ((bf16[16,8,16,1,1,136]{5,2,1,4,3,0:T(8,128)(2,1)}), bf16[16,8,16,1,1,136]{5,2,1,4,3,0:T(8,128)(2,1)S(1)}, u32[]{:S(2)}, u32[]{:S(2)}) async-start(bf16[16,8,16,1,1,136]{5,2,1,4,3,0:T(8,128)(2,1)} %fusion.6), calls=%async_computation.2 | async-start | bytes 2097152 | tf_op jit(solution)/shard_map/all_to_all | solution.py:29
  153.1 50.3 %all-reduce.5.cloned.1.call-start = ((), (), s32[]{:S(2)}) async-start(), calls=%async_computation.6 | async-start | bytes 1048576 | tf_op jit(solution)/shard_map/psum | solution.py:39
  158.0 98.8 %all-gather.2.cloned.1.call-start = ((), (), s32[]{:S(2)}) async-start(), calls=%async_computation.4 | async-start | bytes 5242880 | tf_op jit(solution)/shard_map/all_gather | solution.py:34
  203.4 6.9 %copy-start.1 = (f32[8,16,16,1,136]{4,1,2,0,3:T(8,128)S(1)}, f32[8,16,16,1,136]{4,1,2,0,3:T(8,128)}, u32[]{:S(2)}) copy-start(f32[8,16,16,1,136]{4,1,2,0,3:T(8,128)} %get-tuple-element.22) | copy-start | bytes 3342340
Sparse Core Ops, SparseCore 0:
  14.1 53.1 reduce-scatter.1
  82.4 50.1 all-reduce.2
  158.1 45.2 all-reduce.4
  205.6 51.0 all-gather.1
